TPU v7x, 32 devices: a whole 2x2x4 slice. The times are simulated.
32 devices in a mesh: sub: 8 (over z, x), grp: 4 (over y, core).
Axes of the slice: x: 2, y: 2, z: 4, core: 2. Of those that a mesh axis runs over, the one named last changes fastest.
Arguments:
- resid: float32 [32768, 256], P(('sub', 'grp')), may hold values from -6 to 6
- schur_inv: bfloat16 [65536, 2048], P(('sub', 'grp')), may hold values from -0.125 to 0.125
- basis: bfloat16 [512, 2048], P(('sub', 'grp')), may hold values from -1.5 to 1.5
- scaling: float32 [65536], P(('sub', 'grp')), may hold values from 0.25 to 1
- coarse_inv: bfloat16 [512, 512], P(('sub', 'grp')), may hold values from -0.5 to 0.5
- source_row: int32 [65536], P(('sub', 'grp')), may hold values from 0 to 3071, as said below
- primal_idx: int32 [512], P(('sub', 'grp')), may hold values from 0 to 2047, as said below
Outputs:
- first_apply: float32 [32768, 256], P(('sub', 'grp'))
- second_apply: float32 [32768, 256], P(('sub', 'grp'))
Inputs may be any that keep to these rules, and one draw needn't show every extreme that they name: `source_row`: within one subdomain the entries are distinct; the first subdomain of each chain has none below 1024, the last none at or above 2048. `primal_idx`: within one subdomain the entries are distinct.
All inputs are finite; a program needn't handle non-finite values.
Results may differ from a plain program's by a relative error of at most 0.0076.
Values may be sent and summed in bfloat16 or wider, within the bound.
No kernel may reach another device: no remote copies, remote signals or barrier semaphores. Data moves between devices by JAX's collectives and lax.ppermute only.
A program may use at most 64 MiB of HBM per device.

v0:
```python
import jax
import jax.numpy as jnp
from jax import lax
from jax.sharding import PartitionSpec as P


def with_halo(cells, sides, width):
    for axis, dim in sides:
        count = lax.axis_size(axis)
        ends = count - 1
        head = lax.slice_in_dim(cells, 0, width, axis=dim)
        tail = lax.slice_in_dim(cells, cells.shape[dim] - width, cells.shape[dim], axis=dim)
        cells = jnp.concatenate(
            [
                lax.ppermute(tail, axis, [(i, (i + 1) % count) for i in range(ends)]),
                cells,
                lax.ppermute(head, axis, [((i + 1) % count, i) for i in range(ends)]),
            ],
            axis=dim,
        )
    return cells


def shifted(shard, axis, by):
    devices = lax.axis_size(axis)
    pairs = [(i, i + by) for i in range(devices) if 0 <= i + by < devices]
    return lax.ppermute(shard, axis, pairs)


def shards(resid, schur_inv, basis, scaling, coarse_inv, source_row, primal_idx):
    own_count = resid.shape[0]
    scale_column = scaling[:, None]

    def add_all(portion):
        return jnp.dot(coarse_inv, portion, preferred_element_type=jnp.float32)

    def precondition(vector_in):
        rounded = vector_in.astype(jnp.bfloat16)
        padded = with_halo(rounded, (("sub", 0),), own_count)
        gathered = padded[source_row]
        scaled = (scale_column * gathered.astype(jnp.float32)).astype(jnp.bfloat16)
        primal = scaled[primal_idx]
        idx = lax.axis_index("sub") * lax.axis_size("grp") + lax.axis_index("grp")
        total = lax.axis_size("sub") * lax.axis_size("grp") * primal.shape[0]
        buf = lax.dynamic_update_slice(
            jnp.zeros((total, primal.shape[1]), primal.dtype), primal, (idx * primal.shape[0], 0)
        )
        coarse = add_all(lax.psum(buf, ("sub", "grp")))
        coarse_rounded = coarse.astype(jnp.bfloat16)
        solved = jnp.dot(schur_inv, scaled, preferred_element_type=jnp.float32)
        solved = solved + lax.dot_general(
            basis, coarse_rounded, (((0,), (0,)), ((), ())), preferred_element_type=jnp.float32
        )
        weighted = (scale_column * solved).astype(jnp.bfloat16)
        spread = (
            jnp.zeros((3 * own_count, weighted.shape[1]), jnp.bfloat16).at[source_row].set(weighted)
        )
        from_next = shifted(spread[:own_count], "sub", -1)
        from_previous = shifted(spread[2 * own_count :], "sub", 1)
        return (
            spread[own_count : 2 * own_count].astype(jnp.float32)
            + from_next.astype(jnp.float32)
            + from_previous.astype(jnp.float32)
        )

    first_apply = precondition(resid)
    second_apply = precondition(first_apply)
    return (first_apply, second_apply)


def solution(mesh):
    return jax.shard_map(
        shards,
        mesh=mesh,
        in_specs=(
            P(("sub", "grp"), None),
            P(("sub", "grp"), None),
            P(("sub", "grp"), None),
            P(("sub", "grp")),
            P(("sub", "grp"), None),
            P(("sub", "grp")),
            P(("sub", "grp")),
        ),
        out_specs=(P(("sub", "grp"), None), P(("sub", "grp"), None)),
        check_vma=False,
    )
```

profile of v0, /device:TPU:0, one launch (start us, length us, event | category | flops | bytes accessed | tf_op | source)
XLA Modules:
  0.0 418.4 jit_solution(4887360545982959692)
XLA Ops:
  8.5 1.3 collective-permute-start.1
  9.8 5.5 %collective-permute-start = (bf16[1024,256]{1,0:T(8,128)(2,1)S(1)}, bf16[1024,256]{1,0:T(8,128)(2,1)S(1)}, u32[]{:S(2)}, u32[]{:S(2)}) collective-permute-start(bf16[1024,256]{1,0:T(8,128)(2,1)S(1)} %convert_element_type.56), channel_id=1, source_target_pairs={{0,4},{4,8},{8,12},{12,16},{16,20},{20,24},{24,28},{1,5},{5,9},{9,... | collective-permute-start | bytes 1572872 | tf_op jit(solution)/shard_map/ppermute | solution.py:15
  16.7 8.6 %collective-permute-done.1 = bf16[1024,256]{1,0:T(8,128)(2,1)S(1)} collective-permute-done((bf16[1024,256]{1,0:T(8,128)(2,1)S(1)}, bf16[1024,256]{1,0:T(8,128)(2,1)S(1)}, u32[]{:S(2)}, u32[]{:S(2)}) %collective-permute-start.1) | collective-permute-done | bytes 524320 | tf_op jit(solution)/shard_map/ppermute | solution.py:17
  25.3 11.4 %collective-permute-done = bf16[1024,256]{1,0:T(8,128)(2,1)S(1)} collective-permute-done((bf16[1024,256]{1,0:T(8,128)(2,1)S(1)}, bf16[1024,256]{1,0:T(8,128)(2,1)S(1)}, u32[]{:S(2)}, u32[]{:S(2)}) %collective-permute-start) | collective-permute-done | bytes 524320 | tf_op jit(solution)/shard_map/ppermute | solution.py:15
  36.8 7.5 %gather_fusion = bf16[2048,256]{1,0:T(8,128)(2,1)S(1)} fusion(bf16[3072,256]{1,0:T(8,128)(2,1)S(1)} %pad_maximum_fusion, s32[2048]{0:T(1024)S(1)} %get-tuple-element.8), kind=kCustom, calls=%fused_computation | custom fusion | bytes 2105344 | tf_op jit(solution)/shard_map/gather | solution.py:40
  46.1 5.8 %fusion.13 = f32[256,2048]{1,0:T(8,128)S(1)} fusion(bf16[2048,256]{1,0:T(8,128)(2,1)S(1)} %multiply_convert_fusion.1, bf16[2048,2048]{1,0:T(8,128)(2,1)} %param.8), kind=kOutput, calls=%fused_computation.35 | convolution fusion | flops 2147483648 | bytes 11534336 | tf_op jit(solution)/shard_map/dot_general | solution.py:50
  51.8 120.6 %all-reduce.3.cloned.1.call-done = bf16[512,256]{1,0:T(8,128)(2,1)} async-done(((bf16[512,256]{1,0:T(8,128)(2,1)}), bf16[512,256]{1,0:T(8,128)(2,1)}) %all-reduce.3.cloned.1.call-update) | async-done | bytes 262160 | tf_op jit(solution)/shard_map/psum | solution.py:48
  172.4 1.7 fusion.5
  174.6 9.8 %scatter_custom_fusion = bf16[3072,256]{1,0:T(8,128)(2,1)S(1)} fusion(s32[2048]{0:T(1024)S(1)} %get-tuple-element.9, bf16[2048,256]{1,0:T(8,128)(2,1)S(1)} %copy.9, bf16[]{:T(256)} %constant.10.clone.1), kind=kCustom, calls=%fused_computation.24 | custom fusion | bytes 1572866 | tf_op jit(solution)/shard_map/scatter | solution.py:56
  184.5 1.3 collective-permute-start.2
  185.8 4.6 %collective-permute-start.3 = (bf16[1024,256]{1,0:T(8,128)(2,1)S(1)}, bf16[1024,256]{1,0:T(8,128)(2,1)S(1)}, u32[]{:S(2)}, u32[]{:S(2)}) collective-permute-start(bf16[1024,256]{1,0:T(8,128)(2,1)S(1)} %get-tuple-element.7), channel_id=1, source_target_pairs={{0,4},{4,8},{8,12},{12,16},{16,20},{20,24},{24,28},{1,5},{5,9},{9,... | collective-permute-start | bytes 1572872 | tf_op jit(solution)/shard_map/ppermute | solution.py:27
  190.4 8.9 %collective-permute-done.2 = bf16[1024,256]{1,0:T(8,128)(2,1)S(1)} collective-permute-done((bf16[1024,256]{1,0:T(8,128)(2,1)S(1)}, bf16[1024,256]{1,0:T(8,128)(2,1)S(1)}, u32[]{:S(2)}, u32[]{:S(2)}) %collective-permute-start.2) | collective-permute-done | bytes 524320 | tf_op jit(solution)/shard_map/ppermute | solution.py:27
  199.3 11.1 %collective-permute-done.3 = bf16[1024,256]{1,0:T(8,128)(2,1)S(1)} collective-permute-done((bf16[1024,256]{1,0:T(8,128)(2,1)S(1)}, bf16[1024,256]{1,0:T(8,128)(2,1)S(1)}, u32[]{:S(2)}, u32[]{:S(2)}) %collective-permute-start.3) | collective-permute-done | bytes 524320 | tf_op jit(solution)/shard_map/ppermute | solution.py:27
  212.8 5.2 %collective-permute-start.4 = (bf16[1024,256]{1,0:T(8,128)(2,1)S(1)}, bf16[1024,256]{1,0:T(8,128)(2,1)S(1)}, u32[]{:S(2)}, u32[]{:S(2)}) collective-permute-start(bf16[1024,256]{1,0:T(8,128)(2,1)S(1)} %get-tuple-element.2), channel_id=1, source_target_pairs={{0,4},{4,8},{8,12},{12,16},{16,20},{20,24},{24,28},{1,5},{5,9},{9,... | collective-permute-start | bytes 1572872 | tf_op jit(solution)/shard_map/ppermute | solution.py:15
  218.0 10.0 %collective-permute-done.5 = bf16[1024,256]{1,0:T(8,128)(2,1)S(1)} collective-permute-done((bf16[1024,256]{1,0:T(8,128)(2,1)S(1)}, bf16[1024,256]{1,0:T(8,128)(2,1)S(1)}, u32[]{:S(2)}, u32[]{:S(2)}) %collective-permute-start.5) | collective-permute-done | bytes 524320 | tf_op jit(solution)/shard_map/ppermute | solution.py:17
  228.0 11.4 %collective-permute-done.4 = bf16[1024,256]{1,0:T(8,128)(2,1)S(1)} collective-permute-done((bf16[1024,256]{1,0:T(8,128)(2,1)S(1)}, bf16[1024,256]{1,0:T(8,128)(2,1)S(1)}, u32[]{:S(2)}, u32[]{:S(2)}) %collective-permute-start.4) | collective-permute-done | bytes 524320 | tf_op jit(solution)/shard_map/ppermute | solution.py:15
  239.5 7.5 %gather_fusion.2 = bf16[2048,256]{1,0:T(8,128)(2,1)S(1)} fusion(bf16[3072,256]{1,0:T(8,128)(2,1)S(1)} %pad_maximum_fusion.1, s32[2048]{0:T(1024)S(1)} %get-tuple-element.8), kind=kCustom, calls=%fused_computation.2 | custom fusion | bytes 2105344 | tf_op jit(solution)/shard_map/gather | solution.py:40
  248.7 5.8 %fusion.14 = f32[256,2048]{1,0:T(8,128)S(1)} fusion(bf16[2048,256]{1,0:T(8,128)(2,1)S(1)} %multiply_convert_fusion, bf16[2048,2048]{1,0:T(8,128)(2,1)} %param.8), kind=kOutput, calls=%fused_computation.36 | convolution fusion | flops 2147483648 | bytes 11534336 | tf_op jit(solution)/shard_map/dot_general | solution.py:50
  254.5 118.0 %all-reduce.5.cloned.1.call-done = bf16[512,256]{1,0:T(8,128)(2,1)} async-done(((bf16[512,256]{1,0:T(8,128)(2,1)}), bf16[512,256]{1,0:T(8,128)(2,1)}) %all-reduce.5.cloned.1.call-update) | async-done | bytes 262160 | tf_op jit(solution)/shard_map/psum | solution.py:48
  372.5 1.7 fusion.4
  374.7 9.8 %scatter_custom_fusion.1 = bf16[3072,256]{1,0:T(8,128)(2,1)S(1)} fusion(s32[2048]{0:T(1024)S(1)} %get-tuple-element.9, bf16[2048,256]{1,0:T(8,128)(2,1)S(1)} %copy.10, bf16[]{:T(256)} %constant.10.clone.1), kind=kCustom, calls=%fused_computation.22 | custom fusion | bytes 1572866 | tf_op jit(solution)/shard_map/scatter | solution.py:56
  385.8 4.6 %collective-permute-start.7 = (bf16[1024,256]{1,0:T(8,128)(2,1)S(1)}, bf16[1024,256]{1,0:T(8,128)(2,1)S(1)}, u32[]{:S(2)}, u32[]{:S(2)}) collective-permute-start(bf16[1024,256]{1,0:T(8,128)(2,1)S(1)} %get-tuple-element.5), channel_id=1, source_target_pairs={{0,4},{4,8},{8,12},{12,16},{16,20},{20,24},{24,28},{1,5},{5,9},{9,... | collective-permute-start | bytes 1572872 | tf_op jit(solution)/shard_map/ppermute | solution.py:27
  390.4 8.9 %collective-permute-done.6 = bf16[1024,256]{1,0:T(8,128)(2,1)S(1)} collective-permute-done((bf16[1024,256]{1,0:T(8,128)(2,1)S(1)}, bf16[1024,256]{1,0:T(8,128)(2,1)S(1)}, u32[]{:S(2)}, u32[]{:S(2)}) %collective-permute-start.6) | collective-permute-done | bytes 524320 | tf_op jit(solution)/shard_map/ppermute | solution.py:27
  399.3 11.1 %collective-permute-done.7 = bf16[1024,256]{1,0:T(8,128)(2,1)S(1)} collective-permute-done((bf16[1024,256]{1,0:T(8,128)(2,1)S(1)}, bf16[1024,256]{1,0:T(8,128)(2,1)S(1)}, u32[]{:S(2)}, u32[]{:S(2)}) %collective-permute-start.7) | collective-permute-done | bytes 524320 | tf_op jit(solution)/shard_map/ppermute | solution.py:27
  (36 shorter events, 12.4 us)
Async XLA Ops:
  7.2 165.2 %copy-start = (bf16[16,2048]{1,0:T(8,128)(2,1)S(1)}, bf16[16,2048]{1,0:T(8,128)(2,1)}, u32[]{:S(2)}) copy-start(bf16[16,2048]{1,0:T(8,128)(2,1)} %param.9) | copy-start | bytes 196612
  7.2 165.2 %all-reduce.3.cloned.1.call-start = ((), (), s32[]{:S(2)}) async-start(), calls=%async_computation | async-start | bytes 524288 | tf_op jit(solution)/shard_map/psum | solution.py:48
  8.5 16.8 %collective-permute-start.1 = (bf16[1024,256]{1,0:T(8,128)(2,1)S(1)}, bf16[1024,256]{1,0:T(8,128)(2,1)S(1)}, u32[]{:S(2)}, u32[]{:S(2)}) collective-permute-start(bf16[1024,256]{1,0:T(8,128)(2,1)S(1)} %convert_element_type.56), channel_id=1, source_target_pairs={{4,0},{8,4},{12,8},{16,12},{20,16},{24,20},{28,24},{5,1},{9,5},{13... | collective-permute-start | bytes 1572872 | tf_op jit(solution)/shard_map/ppermute | solution.py:17
  9.8 26.8 %collective-permute-start = (bf16[1024,256]{1,0:T(8,128)(2,1)S(1)}, bf16[1024,256]{1,0:T(8,128)(2,1)S(1)}, u32[]{:S(2)}, u32[]{:S(2)}) collective-permute-start(bf16[1024,256]{1,0:T(8,128)(2,1)S(1)} %convert_element_type.56), channel_id=1, source_target_pairs={{0,4},{4,8},{8,12},{12,16},{16,20},{20,24},{24,28},{1,5},{5,9},{9,... | collective-permute-start | bytes 1572872 | tf_op jit(solution)/shard_map/ppermute | solution.py:15
  36.8 7.5 %copy-start.3 = (f32[2048]{0:T(1024)S(1)}, f32[2048]{0:T(1024)}, u32[]{:S(2)}) copy-start(f32[2048]{0:T(1024)} %param.10) | copy-start | bytes 24580
  45.3 0.7 copy-start.2
  46.0 126.4 %copy-start.4 = (bf16[16,512]{1,0:T(8,128)(2,1)S(1)}, bf16[16,512]{1,0:T(8,128)(2,1)}, u32[]{:S(2)}) copy-start(bf16[16,512]{1,0:T(8,128)(2,1)} %param.11) | copy-start | bytes 49156
  46.0 326.5 %all-reduce.5.cloned.1.call-start = ((), (), s32[]{:S(2)}) async-start(), calls=%async_computation.1 | async-start | bytes 524288 | tf_op jit(solution)/shard_map/psum | solution.py:48
  184.5 14.8 %collective-permute-start.2 = (bf16[1024,256]{1,0:T(8,128)(2,1)S(1)}, bf16[1024,256]{1,0:T(8,128)(2,1)S(1)}, u32[]{:S(2)}, u32[]{:S(2)}) collective-permute-start(bf16[1024,256]{1,0:T(8,128)(2,1)S(1)} %get-tuple-element.6), channel_id=1, source_target_pairs={{4,0},{8,4},{12,8},{16,12},{20,16},{24,20},{28,24},{5,1},{9,5},{13... | collective-permute-start | bytes 1572872 | tf_op jit(solution)/shard_map/ppermute | solution.py:27
  185.8 24.6 %collective-permute-start.3 = (bf16[1024,256]{1,0:T(8,128)(2,1)S(1)}, bf16[1024,256]{1,0:T(8,128)(2,1)S(1)}, u32[]{:S(2)}, u32[]{:S(2)}) collective-permute-start(bf16[1024,256]{1,0:T(8,128)(2,1)S(1)} %get-tuple-element.7), channel_id=1, source_target_pairs={{0,4},{4,8},{8,12},{12,16},{16,20},{20,24},{24,28},{1,5},{5,9},{9,... | collective-permute-start | bytes 1572872 | tf_op jit(solution)/shard_map/ppermute | solution.py:27
  211.5 16.5 %collective-permute-start.5 = (bf16[1024,256]{1,0:T(8,128)(2,1)S(1)}, bf16[1024,256]{1,0:T(8,128)(2,1)S(1)}, u32[]{:S(2)}, u32[]{:S(2)}) collective-permute-start(bf16[1024,256]{1,0:T(8,128)(2,1)S(1)} %get-tuple-element.2), channel_id=1, source_target_pairs={{4,0},{8,4},{12,8},{16,12},{20,16},{24,20},{28,24},{5,1},{9,5},{13... | collective-permute-start | bytes 1572872 | tf_op jit(solution)/shard_map/ppermute | solution.py:17
  212.8 26.6 %collective-permute-start.4 = (bf16[1024,256]{1,0:T(8,128)(2,1)S(1)}, bf16[1024,256]{1,0:T(8,128)(2,1)S(1)}, u32[]{:S(2)}, u32[]{:S(2)}) collective-permute-start(bf16[1024,256]{1,0:T(8,128)(2,1)S(1)} %get-tuple-element.2), channel_id=1, source_target_pairs={{0,4},{4,8},{8,12},{12,16},{16,20},{20,24},{24,28},{1,5},{5,9},{9,... | collective-permute-start | bytes 1572872 | tf_op jit(solution)/shard_map/ppermute | solution.py:15
  248.0 0.7 copy-start.1
  384.5 14.8 %collective-permute-start.6 = (bf16[1024,256]{1,0:T(8,128)(2,1)S(1)}, bf16[1024,256]{1,0:T(8,128)(2,1)S(1)}, u32[]{:S(2)}, u32[]{:S(2)}) collective-permute-start(bf16[1024,256]{1,0:T(8,128)(2,1)S(1)} %get-tuple-element.4), channel_id=1, source_target_pairs={{4,0},{8,4},{12,8},{16,12},{20,16},{24,20},{28,24},{5,1},{9,5},{13... | collective-permute-start | bytes 1572872 | tf_op jit(solution)/shard_map/ppermute | solution.py:27
  385.8 24.6 %collective-permute-start.7 = (bf16[1024,256]{1,0:T(8,128)(2,1)S(1)}, bf16[1024,256]{1,0:T(8,128)(2,1)S(1)}, u32[]{:S(2)}, u32[]{:S(2)}) collective-permute-start(bf16[1024,256]{1,0:T(8,128)(2,1)S(1)} %get-tuple-element.5), channel_id=1, source_target_pairs={{0,4},{4,8},{8,12},{12,16},{16,20},{20,24},{24,28},{1,5},{5,9},{9,... | collective-permute-start | bytes 1572872 | tf_op jit(solution)/shard_map/ppermute | solution.py:27
Sparse Core Ops, SparseCore 0:
  46.1 126.2 all-reduce.2
  248.8 123.6 all-reduce.4
where the time goes:
time: 419 us; the launch traced here: 418 us
  waiting for transfers between devices  320 us (76%)
  local copies, waits for them, and re-layouts  38.4 us (9%)
  starting transfers between devices  25.1 us (6%)
  matrix products  14.9 us (4%)
  between operations  14.3 us (3%)
  other arithmetic  5.82 us (1%)
    psum x2, waiting for transfers between devices, precondition(): coarse = add_all(lax.psum(buf, ('sub', 'grp')))  239 us
    ppermute x4, waiting for transfers between devices, shifted(): return lax.ppermute(shard, axis, pairs)  40 us
    ppermute x2, waiting for transfers between devices, with_halo(): lax.ppermute(tail, axis, [(i, (i + 1) % count) for i in range(ends)])  22.8 us
    scatter x2, local copies, waits for them, and re-layouts, precondition(): jnp.zeros((3 * own_count, weighted.shape[1]), jnp.bfloat16).at[source_row]  19.6 us
    ppermute x2, waiting for transfers between devices, with_halo(): lax.ppermute(head, axis, [((i + 1) % count, i) for i in range(ends)])  18.5 us
    gather x2, local copies, waits for them, and re-layouts, precondition(): gathered = padded[source_row]  15 us
    ppermute x4, starting transfers between devices, shifted(): return lax.ppermute(shard, axis, pairs)  11.7 us
    dot_general x2, matrix products, precondition(): solved = jnp.dot(schur_inv, scaled, preferred_element_type=jnp.float32)  11.5 us
  transfers between devices with their start and end apart: 10, of which 10 were waited for; matrix products, arithmetic and copies ran while one was open for 3% of the time, Pallas kernels for 0%

commit v1 on v0

--- a/solution.py
+++ b/solution.py
@@ -45,7 +45,7 @@
         buf = lax.dynamic_update_slice(
             jnp.zeros((total, primal.shape[1]), primal.dtype), primal, (idx * primal.shape[0], 0)
         )
-        coarse = add_all(lax.psum(buf, ("sub", "grp")))
+        coarse = add_all(lax.psum(lax.psum(buf, "grp"), "sub"))
         coarse_rounded = coarse.astype(jnp.bfloat16)
         solved = jnp.dot(schur_inv, scaled, preferred_element_type=jnp.float32)
         solved = solved + lax.dot_general(

time: 419 us -> 380 us (0.907)
  waiting for transfers between devices: 320 us -> 281 us
    psum x2 -> x4, waiting for transfers between devices: 239 us -> 203 us  [precondition(): coarse = add_all(lax.psum(lax.psum(buf, 'grp'), 'sub'))]
  transfers between devices with their start and end apart: 10 -> 12, of which waited for: 10 -> 12; matrix products, arithmetic and copies ran while one was open for 3% -> 3% of each run, Pallas kernels for 0% -> 0%
where the time goes in v1:
time: 380 us; the launch traced here: 379 us
  waiting for transfers between devices  281 us (74%)
  local copies, waits for them, and re-layouts  38.4 us (10%)
  starting transfers between devices  25.2 us (7%)
  matrix products  14.9 us (4%)
  between operations  14 us (4%)
  other arithmetic  5.83 us (2%)
    psum x4, waiting for transfers between devices, precondition(): coarse = add_all(lax.psum(lax.psum(buf, 'grp'), 'sub'))  203 us
    ppermute x4, waiting for transfers between devices, shifted(): return lax.ppermute(shard, axis, pairs)  36.5 us
    ppermute x2, waiting for transfers between devices, with_halo(): lax.ppermute(tail, axis, [(i, (i + 1) % count) for i in range(ends)])  22.8 us
    scatter x2, local copies, waits for them, and re-layouts, precondition(): jnp.zeros((3 * own_count, weighted.shape[1]), jnp.bfloat16).at[source_row]  19.6 us
    ppermute x2, waiting for transfers between devices, with_halo(): lax.ppermute(head, axis, [((i + 1) % count, i) for i in range(ends)])  18.7 us
    gather x2, local copies, waits for them, and re-layouts, precondition(): gathered = padded[source_row]  15 us
    ppermute x4, starting transfers between devices, shifted(): return lax.ppermute(shard, axis, pairs)  11.7 us
    dot_general x2, matrix products, precondition(): solved = jnp.dot(schur_inv, scaled, preferred_element_type=jnp.float32)  11.5 us
  transfers between devices with their start and end apart: 12, of which 12 were waited for; matrix products, arithmetic and copies ran while one was open for 3% of the time, Pallas kernels for 0%

profile of v1, /device:TPU:0, one launch (start us, length us, event | category | flops | bytes accessed | tf_op | source)
XLA Modules:
  0.0 379.2 jit_solution(13484966933879540861)
XLA Ops:
  9.8 5.5 %collective-permute-start = (bf16[1024,256]{1,0:T(8,128)(2,1)S(1)}, bf16[1024,256]{1,0:T(8,128)(2,1)S(1)}, u32[]{:S(2)}, u32[]{:S(2)}) collective-permute-start(bf16[1024,256]{1,0:T(8,128)(2,1)S(1)} %convert_element_type.56), channel_id=1, source_target_pairs={{0,4},{4,8},{8,12},{12,16},{16,20},{20,24},{24,28},{1,5},{5,9},{9,... | collective-permute-start | bytes 1572872 | tf_op jit(solution)/shard_map/ppermute | solution.py:15
  16.7 8.6 %collective-permute-done.1 = bf16[1024,256]{1,0:T(8,128)(2,1)S(1)} collective-permute-done((bf16[1024,256]{1,0:T(8,128)(2,1)S(1)}, bf16[1024,256]{1,0:T(8,128)(2,1)S(1)}, u32[]{:S(2)}, u32[]{:S(2)}) %collective-permute-start.1) | collective-permute-done | bytes 524320 | tf_op jit(solution)/shard_map/ppermute | solution.py:17
  25.3 11.4 %collective-permute-done = bf16[1024,256]{1,0:T(8,128)(2,1)S(1)} collective-permute-done((bf16[1024,256]{1,0:T(8,128)(2,1)S(1)}, bf16[1024,256]{1,0:T(8,128)(2,1)S(1)}, u32[]{:S(2)}, u32[]{:S(2)}) %collective-permute-start) | collective-permute-done | bytes 524320 | tf_op jit(solution)/shard_map/ppermute | solution.py:15
  36.8 7.5 %gather_fusion = bf16[2048,256]{1,0:T(8,128)(2,1)S(1)} fusion(bf16[3072,256]{1,0:T(8,128)(2,1)S(1)} %pad_maximum_fusion, s32[2048]{0:T(1024)S(1)} %get-tuple-element.8), kind=kCustom, calls=%fused_computation | custom fusion | bytes 2105344 | tf_op jit(solution)/shard_map/gather | solution.py:40
  46.0 33.3 %all-reduce.5.cloned.1.call-done = bf16[512,256]{1,0:T(8,128)(2,1)} async-done(((bf16[512,256]{1,0:T(8,128)(2,1)}), bf16[512,256]{1,0:T(8,128)(2,1)}) %all-reduce.5.cloned.1.call-update) | async-done | bytes 262160 | tf_op jit(solution)/shard_map/psum | solution.py:48
  79.4 5.8 %fusion.13 = f32[256,2048]{1,0:T(8,128)S(1)} fusion(bf16[2048,256]{1,0:T(8,128)(2,1)S(1)} %multiply_convert_fusion.1, bf16[2048,2048]{1,0:T(8,128)(2,1)} %param.8), kind=kOutput, calls=%fused_computation.35 | convolution fusion | flops 2147483648 | bytes 11534336 | tf_op jit(solution)/shard_map/dot_general | solution.py:50
  85.2 68.4 %all-reduce.7.cloned.1.call-done = bf16[512,256]{1,0:T(8,128)(2,1)} async-done(((bf16[512,256]{1,0:T(8,128)(2,1)}), bf16[512,256]{1,0:T(8,128)(2,1)}) %all-reduce.7.cloned.1.call-update) | async-done | bytes 262160 | tf_op jit(solution)/shard_map/psum | solution.py:48
  153.7 1.7 fusion.5
  155.9 9.8 %scatter_custom_fusion = bf16[3072,256]{1,0:T(8,128)(2,1)S(1)} fusion(s32[2048]{0:T(1024)S(1)} %get-tuple-element.9, bf16[2048,256]{1,0:T(8,128)(2,1)S(1)} %copy.9, bf16[]{:T(256)} %constant.10.clone.1), kind=kCustom, calls=%fused_computation.24 | custom fusion | bytes 1572866 | tf_op jit(solution)/shard_map/scatter | solution.py:56
  167.0 4.6 %collective-permute-start.3 = (bf16[1024,256]{1,0:T(8,128)(2,1)S(1)}, bf16[1024,256]{1,0:T(8,128)(2,1)S(1)}, u32[]{:S(2)}, u32[]{:S(2)}) collective-permute-start(bf16[1024,256]{1,0:T(8,128)(2,1)S(1)} %get-tuple-element.7), channel_id=1, source_target_pairs={{0,4},{4,8},{8,12},{12,16},{16,20},{20,24},{24,28},{1,5},{5,9},{9,... | collective-permute-start | bytes 1572872 | tf_op jit(solution)/shard_map/ppermute | solution.py:27
  171.6 7.9 %collective-permute-done.2 = bf16[1024,256]{1,0:T(8,128)(2,1)S(1)} collective-permute-done((bf16[1024,256]{1,0:T(8,128)(2,1)S(1)}, bf16[1024,256]{1,0:T(8,128)(2,1)S(1)}, u32[]{:S(2)}, u32[]{:S(2)}) %collective-permute-start.2) | collective-permute-done | bytes 524320 | tf_op jit(solution)/shard_map/ppermute | solution.py:27
  179.5 10.4 %collective-permute-done.3 = bf16[1024,256]{1,0:T(8,128)(2,1)S(1)} collective-permute-done((bf16[1024,256]{1,0:T(8,128)(2,1)S(1)}, bf16[1024,256]{1,0:T(8,128)(2,1)S(1)}, u32[]{:S(2)}, u32[]{:S(2)}) %collective-permute-start.3) | collective-permute-done | bytes 524320 | tf_op jit(solution)/shard_map/ppermute | solution.py:27
  192.3 5.0 %collective-permute-start.4 = (bf16[1024,256]{1,0:T(8,128)(2,1)S(1)}, bf16[1024,256]{1,0:T(8,128)(2,1)S(1)}, u32[]{:S(2)}, u32[]{:S(2)}) collective-permute-start(bf16[1024,256]{1,0:T(8,128)(2,1)S(1)} %get-tuple-element.2), channel_id=1, source_target_pairs={{0,4},{4,8},{8,12},{12,16},{16,20},{20,24},{24,28},{1,5},{5,9},{9,... | collective-permute-start | bytes 1572872 | tf_op jit(solution)/shard_map/ppermute | solution.py:15
  197.3 10.1 %collective-permute-done.5 = bf16[1024,256]{1,0:T(8,128)(2,1)S(1)} collective-permute-done((bf16[1024,256]{1,0:T(8,128)(2,1)S(1)}, bf16[1024,256]{1,0:T(8,128)(2,1)S(1)}, u32[]{:S(2)}, u32[]{:S(2)}) %collective-permute-start.5) | collective-permute-done | bytes 524320 | tf_op jit(solution)/shard_map/ppermute | solution.py:17
  207.5 11.4 %collective-permute-done.4 = bf16[1024,256]{1,0:T(8,128)(2,1)S(1)} collective-permute-done((bf16[1024,256]{1,0:T(8,128)(2,1)S(1)}, bf16[1024,256]{1,0:T(8,128)(2,1)S(1)}, u32[]{:S(2)}, u32[]{:S(2)}) %collective-permute-start.4) | collective-permute-done | bytes 524320 | tf_op jit(solution)/shard_map/ppermute | solution.py:15
  219.0 7.5 %gather_fusion.2 = bf16[2048,256]{1,0:T(8,128)(2,1)S(1)} fusion(bf16[3072,256]{1,0:T(8,128)(2,1)S(1)} %pad_maximum_fusion.1, s32[2048]{0:T(1024)S(1)} %get-tuple-element.8), kind=kCustom, calls=%fused_computation.2 | custom fusion | bytes 2105344 | tf_op jit(solution)/shard_map/gather | solution.py:40
  228.4 32.8 %all-reduce.9.cloned.1.call-done = bf16[512,256]{1,0:T(8,128)(2,1)} async-done(((bf16[512,256]{1,0:T(8,128)(2,1)}), bf16[512,256]{1,0:T(8,128)(2,1)}) %all-reduce.9.cloned.1.call-update) | async-done | bytes 262160 | tf_op jit(solution)/shard_map/psum | solution.py:48
  261.2 5.8 %fusion.14 = f32[256,2048]{1,0:T(8,128)S(1)} fusion(bf16[2048,256]{1,0:T(8,128)(2,1)S(1)} %multiply_convert_fusion, bf16[2048,2048]{1,0:T(8,128)(2,1)} %param.8), kind=kOutput, calls=%fused_computation.36 | convolution fusion | flops 2147483648 | bytes 11534336 | tf_op jit(solution)/shard_map/dot_general | solution.py:50
  267.0 68.3 %all-reduce.11.cloned.1.call-done = bf16[512,256]{1,0:T(8,128)(2,1)} async-done(((bf16[512,256]{1,0:T(8,128)(2,1)}), bf16[512,256]{1,0:T(8,128)(2,1)}) %all-reduce.11.cloned.1.call-update) | async-done | bytes 262160 | tf_op jit(solution)/shard_map/psum | solution.py:48
  335.3 1.7 fusion.4
  337.5 9.8 %scatter_custom_fusion.1 = bf16[3072,256]{1,0:T(8,128)(2,1)S(1)} fusion(s32[2048]{0:T(1024)S(1)} %get-tuple-element.9, bf16[2048,256]{1,0:T(8,128)(2,1)S(1)} %copy.10, bf16[]{:T(256)} %constant.10.clone.1), kind=kCustom, calls=%fused_computation.22 | custom fusion | bytes 1572866 | tf_op jit(solution)/shard_map/scatter | solution.py:56
  348.7 4.6 %collective-permute-start.7 = (bf16[1024,256]{1,0:T(8,128)(2,1)S(1)}, bf16[1024,256]{1,0:T(8,128)(2,1)S(1)}, u32[]{:S(2)}, u32[]{:S(2)}) collective-permute-start(bf16[1024,256]{1,0:T(8,128)(2,1)S(1)} %get-tuple-element.5), channel_id=1, source_target_pairs={{0,4},{4,8},{8,12},{12,16},{16,20},{20,24},{24,28},{1,5},{5,9},{9,... | collective-permute-start | bytes 1572872 | tf_op jit(solution)/shard_map/ppermute | solution.py:27
  353.3 7.9 %collective-permute-done.6 = bf16[1024,256]{1,0:T(8,128)(2,1)S(1)} collective-permute-done((bf16[1024,256]{1,0:T(8,128)(2,1)S(1)}, bf16[1024,256]{1,0:T(8,128)(2,1)S(1)}, u32[]{:S(2)}, u32[]{:S(2)}) %collective-permute-start.6) | collective-permute-done | bytes 524320 | tf_op jit(solution)/shard_map/ppermute | solution.py:27
  361.1 10.3 %collective-permute-done.7 = bf16[1024,256]{1,0:T(8,128)(2,1)S(1)} collective-permute-done((bf16[1024,256]{1,0:T(8,128)(2,1)S(1)}, bf16[1024,256]{1,0:T(8,128)(2,1)S(1)}, u32[]{:S(2)}, u32[]{:S(2)}) %collective-permute-start.7) | collective-permute-done | bytes 524320 | tf_op jit(solution)/shard_map/ppermute | solution.py:27
  (42 shorter events, 15.2 us)
Async XLA Ops:
  7.2 146.5 %copy-start = (bf16[16,2048]{1,0:T(8,128)(2,1)S(1)}, bf16[16,2048]{1,0:T(8,128)(2,1)}, u32[]{:S(2)}) copy-start(bf16[16,2048]{1,0:T(8,128)(2,1)} %param.9) | copy-start | bytes 196612
  7.2 72.2 %all-reduce.5.cloned.1.call-start = ((), (), s32[]{:S(2)}) async-start(), calls=%async_computation | async-start | bytes 524288 | tf_op jit(solution)/shard_map/psum | solution.py:48
  8.5 16.8 %collective-permute-start.1 = (bf16[1024,256]{1,0:T(8,128)(2,1)S(1)}, bf16[1024,256]{1,0:T(8,128)(2,1)S(1)}, u32[]{:S(2)}, u32[]{:S(2)}) collective-permute-start(bf16[1024,256]{1,0:T(8,128)(2,1)S(1)} %convert_element_type.56), channel_id=1, source_target_pairs={{4,0},{8,4},{12,8},{16,12},{20,16},{24,20},{28,24},{5,1},{9,5},{13... | collective-permute-start | bytes 1572872 | tf_op jit(solution)/shard_map/ppermute | solution.py:17
  9.8 26.8 %collective-permute-start = (bf16[1024,256]{1,0:T(8,128)(2,1)S(1)}, bf16[1024,256]{1,0:T(8,128)(2,1)S(1)}, u32[]{:S(2)}, u32[]{:S(2)}) collective-permute-start(bf16[1024,256]{1,0:T(8,128)(2,1)S(1)} %convert_element_type.56), channel_id=1, source_target_pairs={{0,4},{4,8},{8,12},{12,16},{16,20},{20,24},{24,28},{1,5},{5,9},{9,... | collective-permute-start | bytes 1572872 | tf_op jit(solution)/shard_map/ppermute | solution.py:15
  36.8 7.5 %copy-start.3 = (f32[2048]{0:T(1024)S(1)}, f32[2048]{0:T(1024)}, u32[]{:S(2)}) copy-start(f32[2048]{0:T(1024)} %param.10) | copy-start | bytes 24580
  45.3 0.7 copy-start.2
  46.0 107.7 %all-reduce.7.cloned.1.call-start = ((), (), s32[]{:S(2)}) async-start(), calls=%async_computation.1 | async-start | bytes 524288 | tf_op jit(solution)/shard_map/psum | solution.py:48
  79.4 74.3 %copy-start.4 = (bf16[16,512]{1,0:T(8,128)(2,1)S(1)}, bf16[16,512]{1,0:T(8,128)(2,1)}, u32[]{:S(2)}) copy-start(bf16[16,512]{1,0:T(8,128)(2,1)} %param.11) | copy-start | bytes 49156
  79.4 181.8 %all-reduce.9.cloned.1.call-start = ((), (), s32[]{:S(2)}) async-start(), calls=%async_computation.2 | async-start | bytes 524288 | tf_op jit(solution)/shard_map/psum | solution.py:48
  165.7 13.8 %collective-permute-start.2 = (bf16[1024,256]{1,0:T(8,128)(2,1)S(1)}, bf16[1024,256]{1,0:T(8,128)(2,1)S(1)}, u32[]{:S(2)}, u32[]{:S(2)}) collective-permute-start(bf16[1024,256]{1,0:T(8,128)(2,1)S(1)} %get-tuple-element.6), channel_id=1, source_target_pairs={{4,0},{8,4},{12,8},{16,12},{20,16},{24,20},{28,24},{5,1},{9,5},{13... | collective-permute-start | bytes 1572872 | tf_op jit(solution)/shard_map/ppermute | solution.py:27
  167.0 22.8 %collective-permute-start.3 = (bf16[1024,256]{1,0:T(8,128)(2,1)S(1)}, bf16[1024,256]{1,0:T(8,128)(2,1)S(1)}, u32[]{:S(2)}, u32[]{:S(2)}) collective-permute-start(bf16[1024,256]{1,0:T(8,128)(2,1)S(1)} %get-tuple-element.7), channel_id=1, source_target_pairs={{0,4},{4,8},{8,12},{12,16},{16,20},{20,24},{24,28},{1,5},{5,9},{9,... | collective-permute-start | bytes 1572872 | tf_op jit(solution)/shard_map/ppermute | solution.py:27
  191.0 16.5 %collective-permute-start.5 = (bf16[1024,256]{1,0:T(8,128)(2,1)S(1)}, bf16[1024,256]{1,0:T(8,128)(2,1)S(1)}, u32[]{:S(2)}, u32[]{:S(2)}) collective-permute-start(bf16[1024,256]{1,0:T(8,128)(2,1)S(1)} %get-tuple-element.2), channel_id=1, source_target_pairs={{4,0},{8,4},{12,8},{16,12},{20,16},{24,20},{28,24},{5,1},{9,5},{13... | collective-permute-start | bytes 1572872 | tf_op jit(solution)/shard_map/ppermute | solution.py:17
  192.3 26.6 %collective-permute-start.4 = (bf16[1024,256]{1,0:T(8,128)(2,1)S(1)}, bf16[1024,256]{1,0:T(8,128)(2,1)S(1)}, u32[]{:S(2)}, u32[]{:S(2)}) collective-permute-start(bf16[1024,256]{1,0:T(8,128)(2,1)S(1)} %get-tuple-element.2), channel_id=1, source_target_pairs={{0,4},{4,8},{8,12},{12,16},{16,20},{20,24},{24,28},{1,5},{5,9},{9,... | collective-permute-start | bytes 1572872 | tf_op jit(solution)/shard_map/ppermute | solution.py:15
  227.5 0.7 copy-start.1
  228.2 107.1 %all-reduce.11.cloned.1.call-start = ((), (), s32[]{:S(2)}) async-start(), calls=%async_computation.3 | async-start | bytes 524288 | tf_op jit(solution)/shard_map/psum | solution.py:48
  347.4 13.8 %collective-permute-start.6 = (bf16[1024,256]{1,0:T(8,128)(2,1)S(1)}, bf16[1024,256]{1,0:T(8,128)(2,1)S(1)}, u32[]{:S(2)}, u32[]{:S(2)}) collective-permute-start(bf16[1024,256]{1,0:T(8,128)(2,1)S(1)} %get-tuple-element.4), channel_id=1, source_target_pairs={{4,0},{8,4},{12,8},{16,12},{20,16},{24,20},{28,24},{5,1},{9,5},{13... | collective-permute-start | bytes 1572872 | tf_op jit(solution)/shard_map/ppermute | solution.py:27
  348.7 22.8 %collective-permute-start.7 = (bf16[1024,256]{1,0:T(8,128)(2,1)S(1)}, bf16[1024,256]{1,0:T(8,128)(2,1)S(1)}, u32[]{:S(2)}, u32[]{:S(2)}) collective-permute-start(bf16[1024,256]{1,0:T(8,128)(2,1)S(1)} %get-tuple-element.5), channel_id=1, source_target_pairs={{0,4},{4,8},{8,12},{12,16},{16,20},{20,24},{24,28},{1,5},{5,9},{9,... | collective-permute-start | bytes 1572872 | tf_op jit(solution)/shard_map/ppermute | solution.py:27
Sparse Core Ops, SparseCore 0:
  46.1 33.1 all-reduce.4
  83.1 70.5 all-reduce.6
  228.3 32.8 all-reduce.8
  264.8 70.5 all-reduce.10
